TPU v7x, 32 devices: a whole 2x2x4 slice. The times are simulated.
32 devices in a mesh: dp: 8 (over z, core), ctx: 4 (over y, x).
Axes of the slice: x: 2, y: 2, z: 4, core: 2. Of those that a mesh axis runs over, the one named last changes fastest.
Arguments:
- hidden: bfloat16 [8, 512, 3072], P('dp', 'ctx'), may hold values from -6 to 6
- gating: bfloat16 [8, 512, 3072], P('dp', 'ctx'), may hold values from -6 to 6
- dt_raw: bfloat16 [8, 512, 48], P('dp', 'ctx'), may hold values from -4 to 4
- b_input: bfloat16 [8, 512, 128], P('dp', 'ctx'), may hold values from -0.5 to 0.5
- c_input: bfloat16 [8, 512, 128], P('dp', 'ctx'), may hold values from -0.5 to 0.5
- resets: int32 [8, 2], P('dp'), may hold values 0 or 1
- cotangent: bfloat16 [8, 512, 3072], P('dp', 'ctx'), may hold values from -18 to 18
- parameters: float32 [3216], replicated, may hold values from -10 to 2
- adam_mean: float32 [8, 804], P('dp'), may hold values from -6 to 6
- adam_square: float32 [8, 804], P('dp'), may hold values from 0.1 to 2
- bucket_size: int32 [8], replicated, may hold values from 1 to 804, 3216 in all
- bucket_owner: int32 [8], replicated, may hold values from 0 to 7, each once
Outputs:
- normed: bfloat16 [8, 512, 3072], P('dp', 'ctx')
- grad_hidden: bfloat16 [8, 512, 3072], P('dp', 'ctx')
- grad_gating: bfloat16 [8, 512, 3072], P('dp', 'ctx')
- grad_dt: bfloat16 [8, 512, 48], P('dp', 'ctx')
- grad_b: bfloat16 [8, 512, 128], P('dp', 'ctx')
- grad_c: bfloat16 [8, 512, 128], P('dp', 'ctx')
- new_params: float32 [3216], replicated
- new_mean: float32 [8, 804], P('dp')
- new_square: float32 [8, 804], P('dp')
Inputs may be any that keep to these rules, and one draw needn't show every extreme that they name: `bucket_size`: the sizes sum to 3216; the largest is exactly 804. `bucket_owner`: each dp index owns exactly one bucket.
All inputs are finite; a program needn't handle non-finite values. No bound on the sum of `resets` on one device may be relied on, other than what follows from the above.
Results may differ from a plain program's by a relative error of at most 0.0076.
Values may be sent and summed in bfloat16 or wider, within the bound.
No kernel may reach another device: no remote copies, remote signals or barrier semaphores. Data moves between devices by JAX's collectives and lax.ppermute only.
A program may use at most 128 MiB of HBM per device.

v0:
```python
import jax
import jax.numpy as jnp
from jax import lax
from jax.sharding import PartitionSpec as P

SPAN = 256
CH = 3072
eps_norm = 1e-05
clip_norm = 64.0
beta_one = 0.9
beta_two = 0.95
adam_eps = 1e-08
learn_rate = 0.02
step_count = 100.0
highest = lax.Precision.HIGHEST


def rounded(value):
    return lax.optimization_barrier(value.astype(jnp.bfloat16)).astype(jnp.float32)


def ssd_group(hidden, dt_raw, b_input, c_input, resets, a_log, dt_bias, skip):
    length = hidden.shape[0]
    heads = a_log.shape[0]
    width = hidden.shape[1] // heads
    blocks = length // SPAN
    step_sizes = jax.nn.softplus(dt_raw.astype(jnp.float32) + dt_bias)
    log_decay = (step_sizes * -jnp.exp(a_log)).reshape(blocks, SPAN, heads).transpose(0, 2, 1)
    cumul = jnp.cumsum(log_decay, axis=2)
    inputs = hidden.astype(jnp.float32).reshape(blocks, SPAN, heads, width)
    scaled = rounded(inputs * step_sizes.reshape(blocks, SPAN, heads, 1))
    b_rows = b_input.astype(jnp.float32).reshape(blocks, SPAN, -1)
    c_rows = c_input.astype(jnp.float32).reshape(blocks, SPAN, -1)
    scores = jnp.einsum("ctn,csn->cts", c_rows, b_rows, precision=highest)
    causal = jnp.arange(SPAN)[:, None] >= jnp.arange(SPAN)[None, :]
    spread = cumul[:, :, :, None] - cumul[:, :, None, :]
    decay = jnp.where(causal, jnp.exp(jnp.where(causal, spread, 0.0)), 0.0)
    weights = rounded(scores[:, None] * decay)
    intra = jnp.einsum("chts,cshp->cthp", weights, scaled, precision=highest)
    tail = cumul[:, :, -1:] - cumul
    b_decayed = rounded(b_rows[:, None] * jnp.exp(tail)[..., None])
    block_state = jnp.einsum("chsn,cshp->chnp", b_decayed, scaled, precision=highest)
    keep = 1.0 - resets.astype(jnp.float32)

    def advance(state, items):
        keep_one, total, added = items
        entering = state * keep_one
        return (jnp.exp(total)[:, None, None] * entering + added, entering)

    start_state = jnp.zeros(block_state.shape[1:], jnp.float32)
    last_state, entering = lax.scan(advance, start_state, (keep, cumul[:, :, -1], block_state))
    c_decayed = rounded(c_rows[:, None] * jnp.exp(cumul)[..., None])
    inter = jnp.einsum("chtn,chnp->cthp", c_decayed, rounded(entering), precision=highest)
    output = intra + inter + skip[:, None] * inputs
    return output.reshape(length, heads * width).astype(jnp.bfloat16)


def gate_values(y_values, gating):
    gated = y_values.astype(jnp.float32) * jax.nn.silu(gating.astype(jnp.float32))
    return (gated, jnp.sum(gated * gated, axis=-1))


def normalize(gated, total, gain):
    factor = lax.rsqrt(total / CH + eps_norm)
    return (factor, (gated * factor[..., None] * gain).astype(jnp.bfloat16))


def norm_backward(cotangent, gain, gated, factor, dot_total, y_values, gating):
    upstream = cotangent.astype(jnp.float32) * gain
    d_gated = (
        upstream * factor[..., None]
        - gated * (factor * factor * factor * dot_total / CH)[..., None]
    )
    gate_f = gating.astype(jnp.float32)
    sigma = jax.nn.sigmoid(gate_f)
    d_y = (d_gated * (gate_f * sigma)).astype(jnp.bfloat16)
    d_gate = (
        d_gated * y_values.astype(jnp.float32) * sigma * (1.0 + gate_f * (1.0 - sigma))
    ).astype(jnp.bfloat16)
    d_gain = jnp.sum(
        cotangent.astype(jnp.float32) * gated * factor[..., None], axis=tuple(range(gated.ndim - 1))
    )
    return (d_y, d_gate, d_gain)


def on_device(
    hidden,
    gating,
    dt_raw,
    b_input,
    c_input,
    resets,
    cotangent,
    parameters,
    adam_mean,
    adam_square,
    bucket_size,
    bucket_owner,
):
    heads_all = dt_raw.shape[2]
    groups = lax.axis_size("ctx")
    group = heads_all // groups
    state_size = b_input.shape[2]
    tokens = hidden.shape[1]
    first = lax.axis_index("ctx") * group
    head_params = parameters[: 3 * heads_all].reshape(3, heads_all)
    gain = parameters[3 * heads_all :]
    local_params = lax.dynamic_slice_in_dim(head_params, first, group, 1)
    b_all, c_all = (
        lax.all_gather(b_input, "ctx", axis=1, tiled=True),
        lax.all_gather(c_input, "ctx", axis=1, tiled=True),
    )
    seq_resets = resets[0]
    owners_n = lax.axis_size("dp")
    cap_n = adam_mean.shape[1]
    len_n = parameters.shape[0]
    state_all = lax.all_gather(jnp.stack([adam_mean[0], adam_square[0]]), "dp", axis=0)
    starts = jnp.cumsum(bucket_size) - bucket_size
    laid = jnp.zeros((2, len_n + cap_n), jnp.float32)
    for k in range(owners_n):
        laid = lax.dynamic_update_slice(laid, state_all[bucket_owner[k]], (0, starts[k]))
    mean_flat = laid[0, :len_n]
    square_flat = laid[1, :len_n]

    def local_fn(x_arg, dt_arg, b_arg, c_arg, a_arg, bias_arg, skip_arg):
        return ssd_group(x_arg, dt_arg, b_arg, c_arg, seq_resets, a_arg, bias_arg, skip_arg)

    x_heads, dt_heads = (
        lax.all_to_all(hidden, "ctx", split_axis=2, concat_axis=1, tiled=True),
        lax.all_to_all(dt_raw, "ctx", split_axis=2, concat_axis=1, tiled=True),
    )
    y_heads, pullback = jax.vjp(
        local_fn,
        x_heads[0],
        dt_heads[0],
        b_all[0],
        c_all[0],
        local_params[0],
        local_params[1],
        local_params[2],
    )
    y_seq = lax.all_to_all(y_heads[None], "ctx", split_axis=1, concat_axis=2, tiled=True)
    gated, total = gate_values(y_seq, gating)
    factor, normed = normalize(gated, total, gain)
    dot_total = jnp.sum(cotangent.astype(jnp.float32) * gain * gated, axis=-1)
    d_y, grad_gating, d_gain = norm_backward(
        cotangent, gain, gated, factor, dot_total, y_seq, gating
    )
    d_y_heads = lax.all_to_all(d_y, "ctx", split_axis=2, concat_axis=1, tiled=True)
    d_x, d_dt, d_b, d_c, d_alog, d_bias, d_skip = pullback(d_y_heads[0])
    d_pair = jnp.concatenate([d_b, d_c], axis=-1)
    grad_hidden, grad_dt, pair_parts = (
        lax.all_to_all(d_x[None], "ctx", split_axis=1, concat_axis=2, tiled=True),
        lax.all_to_all(d_dt[None], "ctx", split_axis=1, concat_axis=2, tiled=True),
        lax.all_to_all(d_pair[None], "ctx", split_axis=1, concat_axis=2, tiled=True),
    )
    pair_sum = jnp.sum(
        pair_parts.reshape(1, tokens, groups, 2 * state_size).astype(jnp.float32), axis=2
    ).astype(jnp.bfloat16)
    grad_b = pair_sum[..., :state_size]
    grad_c = pair_sum[..., state_size:]
    head_grads = jnp.stack([d_alog, d_bias, d_skip])
    full_heads = lax.dynamic_update_slice(
        jnp.zeros((3, heads_all), jnp.float32), head_grads, (0, first)
    )
    grad_part = jnp.concatenate([full_heads.reshape(-1), d_gain])
    gradient = lax.psum(grad_part, ("dp", "ctx"))
    grad_norm = jnp.sqrt(jnp.sum(gradient * gradient))
    shrink = jnp.minimum(1.0, clip_norm / (grad_norm + 1e-06))
    owners = lax.axis_size("dp")
    slot_cap = adam_mean.shape[1]
    total_len = parameters.shape[0]
    ends = jnp.cumsum(bucket_size)
    begins = ends - bucket_size
    order = jnp.arange(owners, dtype=jnp.int32)
    mine = lax.axis_index("dp")
    my_bucket = jnp.sum(jnp.where(bucket_owner == mine, order, 0))
    row_begin = jnp.sum(jnp.where(order == my_bucket, begins, 0))
    row_size = jnp.sum(jnp.where(order == my_bucket, bucket_size, 0))
    slots = jnp.arange(slot_cap, dtype=jnp.int32)
    valid = slots < row_size
    padding = jnp.zeros((slot_cap,), jnp.float32)
    grad_row = (
        jnp.where(
            valid,
            lax.dynamic_slice_in_dim(jnp.concatenate([gradient, padding]), row_begin, slot_cap),
            0.0,
        )
        * shrink
    )
    new_mean = beta_one * adam_mean[0] + (1.0 - beta_one) * grad_row
    new_square = beta_two * adam_square[0] + (1.0 - beta_two) * grad_row * grad_row
    grad_flat = gradient * shrink
    mean_all = beta_one * mean_flat + (1.0 - beta_one) * grad_flat
    square_all = beta_two * square_flat + (1.0 - beta_two) * grad_flat * grad_flat
    direction = (
        mean_all
        / (1.0 - beta_one**step_count)
        / (jnp.sqrt(square_all / (1.0 - beta_two**step_count)) + adam_eps)
    )
    new_params = parameters - learn_rate * direction
    return (
        normed,
        grad_hidden,
        grad_gating,
        grad_dt,
        grad_b,
        grad_c,
        new_params,
        new_mean[None],
        new_square[None],
    )


def solution(mesh):
    return jax.shard_map(
        on_device,
        mesh=mesh,
        in_specs=(
            P("dp", "ctx", None),
            P("dp", "ctx", None),
            P("dp", "ctx", None),
            P("dp", "ctx", None),
            P("dp", "ctx", None),
            P("dp", None),
            P("dp", "ctx", None),
            P(),
            P("dp", None),
            P("dp", None),
            P(),
            P(),
        ),
        out_specs=(
            P("dp", "ctx", None),
            P("dp", "ctx", None),
            P("dp", "ctx", None),
            P("dp", "ctx", None),
            P("dp", "ctx", None),
            P("dp", "ctx", None),
            P(),
            P("dp", None),
            P("dp", None),
        ),
        check_vma=False,
    )
```

profile of v0, /device:TPU:0, one launch (start us, length us, event | category | flops | bytes accessed | tf_op | source)
XLA Modules:
  0.0 367.2 jit_solution(14272552152918870720)
XLA Ops:
  3.3 5.2 %all-to-all-start.1 = ((bf16[4,2,768]{2,1,0:T(2,128)(2,1)}), bf16[4,2,768]{2,1,0:T(2,128)(2,1)S(1)}, u32[]{:S(2)}, u32[]{:S(2)}) async-start(bf16[4,2,768]{2,1,0:T(2,128)(2,1)} %reshape.560), calls=%async_computation.1 | async-start | bytes 24576 | tf_op jit(solution)/shard_map/all_to_all | solution.py:130
  10.6 9.1 %all_gather.13 = bf16[1,512,128]{2,1,0:T(8,128)(2,1)S(1)} all-gather(bf16[1,128,128]{2,1,0:T(8,128)(2,1)} %param.19), channel_id=1, replica_groups=mesh['dp'=8,'ctx'=4] {'ctx'}, dimensions={1}, use_global_device_ids=true | all-gather | bytes 163840 | tf_op jit(solution)/shard_map/all_gather | solution.py:110
  19.7 8.2 %all_gather.12 = bf16[1,512,128]{2,1,0:T(8,128)(2,1)S(1)} all-gather(bf16[1,128,128]{2,1,0:T(8,128)(2,1)} %param.20), channel_id=1, replica_groups=mesh['dp'=8,'ctx'=4] {'ctx'}, dimensions={1}, use_global_device_ids=true | all-gather | bytes 163840 | tf_op jit(solution)/shard_map/all_gather | solution.py:111
  28.7 3.8 %copy.220 = bf16[1,128,3072]{1,0,2:T(2,128)(2,1)S(1)} copy(bf16[1,128,3072]{2,1,0:T(8,128)(2,1)} %param.16) | data formatting | bytes 1572864 | tf_op args[0]
  32.5 17.9 %reduce.27 = bf16[3072,128]{1,0:T(8,128)(2,1)} reduce(bf16[3072,1,128]{2,1,0:T(2,128)(2,1)S(1)} %bitcast.223, bf16[]{:T(256)} %broadcast.249), dimensions={1}, to_apply=%bitcast.152.reduce_sub_computation | reduce | bytes 1572866
  52.4 3.7 %all-to-all-start = ((bf16[4,2,49152]{2,1,0:T(2,128)(2,1)}), bf16[4,2,49152]{2,1,0:T(2,128)(2,1)S(1)}, u32[]{:S(2)}, u32[]{:S(2)}) async-start(bf16[4,2,49152]{2,1,0:T(2,128)(2,1)} %reshape.562), calls=%async_computation | async-start | bytes 1572864 | tf_op jit(solution)/shard_map/all_to_all | solution.py:129
  80.9 7.0 %while.36 = (s32[]{:T(128)}, f32[12,128,64]{2,1,0:T(8,128)S(1)}, f32[2,12,128,64]{3,2,1,0:T(8,128)S(1)}, f32[2,12]{1,0:T(2,128)S(1)}, f32[2,12,1,1]{1,3,2,0:T(1,...) while((s32[]{:T(128)}, f32[12,128,64]{2,1,0:T(8,128)S(1)}, ...), condition=%wide.region_3.4_spmd.clone, body=%wide.region_2.3_spmd.clone.sunk | while | flops 589827 | bytes 5899176 | solution.py:51
  96.8 6.4 %reduce.28 = bf16[512,768]{1,0:T(8,128)(2,1)S(1)} reduce(bf16[512,1,768]{2,1,0:T(2,128)(2,1)} %bitcast.217, bf16[]{:T(256)} %broadcast.249), dimensions={1}, to_apply=%bitcast.154.reduce_sub_computation | reduce | bytes 1572866
  104.3 4.2 %all-to-all-start.2 = ((bf16[4,2,49152]{2,1,0:T(2,128)(2,1)}), bf16[4,2,49152]{2,1,0:T(2,128)(2,1)}, u32[]{:S(2)}, u32[]{:S(2)}) async-start(bf16[4,2,49152]{2,1,0:T(2,128)(2,1)} %reshape.564), calls=%async_computation.2 | async-start | bytes 1572864 | tf_op jit(solution)/shard_map/all_to_all | solution.py:142
  125.3 3.7 %reshape.565 = bf16[512,1,768]{2,1,0:T(2,128)(2,1)} reshape(bf16[4,2,49152]{2,1,0:T(2,128)(2,1)} %all-to-all-done.2) | data formatting | bytes 1572864
  140.9 13.0 %copy.372 = bf16[1,128,3072]{1,0,2:T(2,128)(2,1)} copy(bf16[1,128,3072]{1,2,0:T(8,128)(2,1)S(1)} %get-tuple-element.489) | data formatting | bytes 1572864 | tf_op jit(solution)/shard_map/convert_element_type | solution.py:76
  153.9 18.5 %reduce.29 = bf16[3072,128]{1,0:T(8,128)(2,1)S(1)} reduce(bf16[3072,1,128]{2,1,0:T(2,128)(2,1)} %bitcast.219, bf16[]{:T(256)} %broadcast.249), dimensions={1}, to_apply=%bitcast.190.reduce_sub_computation | reduce | bytes 1572866
  173.4 4.1 %all-to-all-start.3 = ((bf16[4,2,49152]{2,1,0:T(2,128)(2,1)}), bf16[4,2,49152]{2,1,0:T(2,128)(2,1)S(1)}, u32[]{:S(2)}, u32[]{:S(2)}) async-start(bf16[4,2,49152]{2,1,0:T(2,128)(2,1)} %reshape.566), calls=%async_computation.3 | async-start | bytes 1572864 | tf_op jit(solution)/shard_map/all_to_all | solution.py:149
  200.0 14.3 %all-gather.1 = f32[8,2,804]{2,1,0:T(2,128)S(1)} all-gather(f32[1,2,804]{2,1,0:T(2,128)S(1)} %maximum_bitcast_fusion.1), channel_id=2, replica_groups=mesh['dp'=8,'ctx'=4] {'dp'}, dimensions={0}, use_global_device_ids=true | all-gather | bytes 57888 | tf_op jit(solution)/shard_map/all_gather | solution.py:117
  242.2 13.7 %while.37 = (s32[]{:T(128)}, f32[12,128,64]{2,1,0:T(8,128)S(1)}, f32[2,12]{1,0:T(2,128)}, f32[2,12,128,64]{3,2,1,0:T(8,128)}, f32[2,12,128,64]{2,3,1,0:T(8,128)}...) while((s32[]{:T(128)}, f32[12,128,64]{2,1,0:T(8,128)S(1)}, ...), condition=%wide.region_8.9_spmd.clone, body=%wide.region_6.8_spmd.clone.sunk | while | flops 688132 | bytes 4327636 | solution.py:51
  255.9 3.8 %fusion.90 = f32[2,12,64,256]{3,2,1,0:T(8,128)S(1)} fusion(f32[2,12,128,64]{3,2,1,0:T(8,128)} %get-tuple-element.236, bf16[2,12,256,128]{3,2,1,0:T(8,128)(2,1)} %multiply_convert_fusion.2), kind=kOutput, calls=%fused_computation.192 | convolution fusion | flops 603979776 | bytes 3932160 | tf_op jit(solution)/shard_map/transpose(jvp(chsn,cshp->chnp))/dot_general | solution.py:42
  266.5 5.7 %fusion.11 = (f32[2,12,256]{2,1,0:T(8,128)S(1)}, f32[2,12,256]{2,1,0:T(8,128)S(1)}, f32[2,256,256]{2,1,0:T(8,128)S(1)}) fusion(bf16[2,12,256,256]{3,2,1,0:T(8,128)(2,1)} %convolution_convert_fusion, f32[2,12,256]{2,1,0:T(8,128)S(1)} %copy-done.36, f32[2,256,256]{2,1,0:T(8,128)S(1)} %copy-done.25, pred[256,256]{1,0:T(8,128)(4,1)S(1)} %copy-done.38), kind=kLoop, calls=%fused_computation.26 | loop fusion | flops 18731008 | bytes 4333568 | tf_op jit(solution)/shard_map/transpose(jvp())/reduce_sum | solution.py:36
  272.4 3.8 %fusion.13 = (f32[2,256,128]{2,1,0:T(8,128)S(1)}, f32[2,12,256]{2,1,0:T(8,128)S(1)}, f32[2,12,256]{2,1,0:T(8,128)S(1)}, f32[2,256,128]{2,1,0:T(8,128)S(1)}) fusion(bf16[2,12,256,128]{3,2,1,0:T(8,128)(2,1)S(1)} %copy-done.22, f32[2,12,256]{2,1,0:T(8,128)S(1)} %copy-done.48, f32[2,256,128]{2,1,0:T(8,128)S(1)} %copy-done.30, f32[2,256,128]{2,1,0:T(8,128)S(1)} %copy-done.28, ...), kind=kLoop, calls=%fused_computation.32 | loop fusion | flops 7720960 | bytes 4292608 | tf_op jit(solution)/shard_map/transpose(jvp())/reduce_sum | solution.py:52
  276.8 5.0 %reduce-window.31 = f32[2,12,2,128]{3,1,2,0:T(8,128)S(1)} reduce-window(f32[2,12,2,128]{3,1,2,0:T(8,128)S(1)} %copy.261, f32[]{:T(128)} %constant.128.clone.1), window={size=1x1x1x128 pad=0_0x0_0x0_0x0_127}, to_apply=%region_15.16 | reduce-window | flops 780288 | bytes 49156 | tf_op jit(solution)/shard_map/reduce-window.2
  285.0 4.2 %all-to-all-start.5 = ((bf16[4,2,768]{2,1,0:T(2,128)(2,1)}), bf16[4,2,768]{2,1,0:T(2,128)(2,1)S(1)}, u32[]{:S(2)}, u32[]{:S(2)}) async-start(bf16[4,2,768]{2,1,0:T(2,128)(2,1)} %reshape.570), calls=%async_computation.5 | async-start | bytes 24576 | tf_op jit(solution)/shard_map/all_to_all | solution.py:154
  294.2 5.5 %reduce.30 = bf16[512,768]{1,0:T(8,128)(2,1)S(1)} reduce(bf16[512,1,768]{2,1,0:T(2,128)(2,1)S(1)} %bitcast.221, bf16[]{:T(256)} %broadcast.249), dimensions={1}, to_apply=%bitcast.158.reduce_sub_computation | reduce | bytes 1572866
  304.2 4.3 %all-to-all-start.6 = ((bf16[4,2,16384]{2,1,0:T(2,128)(2,1)}), bf16[4,2,16384]{2,1,0:T(2,128)(2,1)S(1)}, u32[]{:S(2)}, u32[]{:S(2)}) async-start(bf16[4,2,16384]{2,1,0:T(2,128)(2,1)} %reshape.572), calls=%async_computation.6 | async-start | bytes 524288 | tf_op jit(solution)/shard_map/all_to_all | solution.py:155
  308.6 40.7 %psum.7 = f32[3216]{0:T(1024)S(1)} all-reduce(f32[3216]{0:T(1024)S(1)} %pad_maximum_fusion), channel_id=1, replica_groups=mesh['dp'=8,'ctx'=4] {'dp','ctx'}, use_global_device_ids=true, to_apply=%region_27.28 | all-reduce | flops 3216 | bytes 25728 | tf_op jit(solution)/shard_map/psum | solution.py:167
  358.9 5.6 %all-to-all-done.4 = bf16[4,2,49152]{2,1,0:T(2,128)(2,1)S(1)} async-done(((bf16[4,2,49152]{2,1,0:T(2,128)(2,1)}), bf16[4,2,49152]{2,1,0:T(2,128)(2,1)S(1)}, u32[]{:S(2)}, u32[]{:S(2)}) %all-to-all-start.4) | async-done | bytes 786464 | tf_op jit(solution)/shard_map/all_to_all | solution.py:153
  (356 shorter events, 141.5 us)
Async XLA Ops:
  3.3 49.1 %all-to-all-start.1 = ((bf16[4,2,768]{2,1,0:T(2,128)(2,1)}), bf16[4,2,768]{2,1,0:T(2,128)(2,1)S(1)}, u32[]{:S(2)}, u32[]{:S(2)}) async-start(bf16[4,2,768]{2,1,0:T(2,128)(2,1)} %reshape.560), calls=%async_computation.1 | async-start | bytes 24576 | tf_op jit(solution)/shard_map/all_to_all | solution.py:130
  9.3 23.2 %copy-start.73 = (f32[3,12]{1,0:T(4,128)}, f32[3,12]{1,0:T(4,128)S(1)}, u32[]{:S(2)}) copy-start(f32[3,12]{1,0:T(4,128)S(1)} %constant_dynamic-slice_fusion.4) | copy-start | bytes 436
  9.3 46.8 %copy-start.65 = (f32[12]{0:T(128)}, f32[12]{0:T(128)S(1)}, u32[]{:S(2)}) copy-start(f32[12]{0:T(128)S(1)} %get-tuple-element.511) | copy-start | bytes 148
  9.4 46.9 %copy-start.67 = (f32[12]{0:T(128)}, f32[12]{0:T(128)S(1)}, u32[]{:S(2)}) copy-start(f32[12]{0:T(128)S(1)} %get-tuple-element.512) | copy-start | bytes 148
  9.4 81.3 %copy-start.69 = (f32[12]{0:T(128)}, f32[12]{0:T(128)S(1)}, u32[]{:S(2)}) copy-start(f32[12]{0:T(128)S(1)} %get-tuple-element.510) | copy-start | bytes 148
  28.2 34.7 %copy-start.24 = (f32[2,256,256]{2,1,0:T(8,128)}, f32[2,256,256]{2,1,0:T(8,128)S(1)}, u32[]{:S(2)}) copy-start(f32[2,256,256]{2,1,0:T(8,128)S(1)} %fusion.87) | copy-start | bytes 1572868
  28.2 34.6 %copy-start.37 = (pred[256,256]{1,0:T(8,128)(4,1)}, pred[256,256]{1,0:T(8,128)(4,1)S(1)}, u32[]{:S(2)}) copy-start(pred[256,256]{1,0:T(8,128)(4,1)S(1)} %iota_compare_fusion) | copy-start | bytes 196612
  28.6 30.5 %copy-start.27 = (f32[2,256,128]{2,1,0:T(8,128)}, f32[2,256,128]{2,1,0:T(8,128)S(1)}, u32[]{:S(2)}) copy-start(f32[2,256,128]{2,1,0:T(8,128)S(1)} %convert_element_type.229) | copy-start | bytes 786436
  28.7 32.4 %copy-start.29 = (f32[2,256,128]{2,1,0:T(8,128)}, f32[2,256,128]{2,1,0:T(8,128)S(1)}, u32[]{:S(2)}) copy-start(f32[2,256,128]{2,1,0:T(8,128)S(1)} %convert_element_type.232) | copy-start | bytes 786436
  52.4 13.3 %all-to-all-start = ((bf16[4,2,49152]{2,1,0:T(2,128)(2,1)}), bf16[4,2,49152]{2,1,0:T(2,128)(2,1)S(1)}, u32[]{:S(2)}, u32[]{:S(2)}) async-start(bf16[4,2,49152]{2,1,0:T(2,128)(2,1)} %reshape.562), calls=%async_computation | async-start | bytes 1572864 | tf_op jit(solution)/shard_map/all_to_all | solution.py:129
  56.3 20.6 %copy-start.43 = (f32[2,256,12]{1,2,0:T(8,128)}, f32[2,256,12]{1,2,0:T(8,128)S(1)}, u32[]{:S(2)}) copy-start(f32[2,256,12]{1,2,0:T(8,128)S(1)} %get-tuple-element.503) | copy-start | bytes 73732
  104.3 21.0 %all-to-all-start.2 = ((bf16[4,2,49152]{2,1,0:T(2,128)(2,1)}), bf16[4,2,49152]{2,1,0:T(2,128)(2,1)}, u32[]{:S(2)}, u32[]{:S(2)}) async-start(bf16[4,2,49152]{2,1,0:T(2,128)(2,1)} %reshape.564), calls=%async_computation.2 | async-start | bytes 1572864 | tf_op jit(solution)/shard_map/all_to_all | solution.py:142
  172.4 27.6 %copy-start.63 = (f32[1,804]{1,0:T(1,128)S(1)}, f32[1,804]{1,0:T(1,128)}, u32[]{:S(2)}) copy-start(f32[1,804]{1,0:T(1,128)} %param.25) | copy-start | bytes 9652
  172.4 27.6 %copy-start.64 = (f32[1,804]{1,0:T(1,128)S(1)}, f32[1,804]{1,0:T(1,128)}, u32[]{:S(2)}) copy-start(f32[1,804]{1,0:T(1,128)} %param.24) | copy-start | bytes 9652
  173.4 50.9 %all-to-all-start.3 = ((bf16[4,2,49152]{2,1,0:T(2,128)(2,1)}), bf16[4,2,49152]{2,1,0:T(2,128)(2,1)S(1)}, u32[]{:S(2)}, u32[]{:S(2)}) async-start(bf16[4,2,49152]{2,1,0:T(2,128)(2,1)} %reshape.566), calls=%async_computation.3 | async-start | bytes 1572864 | tf_op jit(solution)/shard_map/all_to_all | solution.py:149
  276.2 13.0 %copy-start.34 = (bf16[1,512,128]{2,1,0:T(8,128)(2,1)S(1)}, bf16[1,512,128]{2,1,0:T(8,128)(2,1)}, u32[]{:S(2)}) copy-start(bf16[1,512,128]{2,1,0:T(8,128)(2,1)} %copy-done.33) | copy-start | bytes 393220
  276.2 13.4 %copy-start.32 = (bf16[1,512,128]{2,1,0:T(8,128)(2,1)S(1)}, bf16[1,512,128]{2,1,0:T(8,128)(2,1)}, u32[]{:S(2)}) copy-start(bf16[1,512,128]{2,1,0:T(8,128)(2,1)} %copy-done.31) | copy-start | bytes 393220
  285.0 19.2 %all-to-all-start.5 = ((bf16[4,2,768]{2,1,0:T(2,128)(2,1)}), bf16[4,2,768]{2,1,0:T(2,128)(2,1)S(1)}, u32[]{:S(2)}, u32[]{:S(2)}) async-start(bf16[4,2,768]{2,1,0:T(2,128)(2,1)} %reshape.570), calls=%async_computation.5 | async-start | bytes 24576 | tf_op jit(solution)/shard_map/all_to_all | solution.py:154
  301.0 53.2 %copy-start.61 = (f32[804]{0:T(1024)S(1)}, f32[804]{0:T(1024)}, u32[]{:S(2)}) copy-start(f32[804]{0:T(1024)} %get-tuple-element.532) | copy-start | bytes 9652
  301.0 53.2 %copy-start.62 = (f32[804]{0:T(1024)S(1)}, f32[804]{0:T(1024)}, u32[]{:S(2)}) copy-start(f32[804]{0:T(1024)} %get-tuple-element.533) | copy-start | bytes 9652
  303.3 52.8 %copy-start.52 = (f32[3216]{0:T(1024)S(1)}, f32[3216]{0:T(1024)}, u32[]{:S(2)}) copy-start(f32[3216]{0:T(1024)} %get-tuple-element.445) | copy-start | bytes 38596
  303.3 52.8 %copy-start.54 = (f32[3216]{0:T(1024)S(1)}, f32[3216]{0:T(1024)}, u32[]{:S(2)}) copy-start(f32[3216]{0:T(1024)} %param.23) | copy-start | bytes 38596
  304.2 46.4 %all-to-all-start.6 = ((bf16[4,2,16384]{2,1,0:T(2,128)(2,1)}), bf16[4,2,16384]{2,1,0:T(2,128)(2,1)S(1)}, u32[]{:S(2)}, u32[]{:S(2)}) async-start(bf16[4,2,16384]{2,1,0:T(2,128)(2,1)} %reshape.572), calls=%async_computation.6 | async-start | bytes 524288 | tf_op jit(solution)/shard_map/all_to_all | solution.py:155
  350.6 13.8 %all-to-all-start.4 = ((bf16[4,2,49152]{2,1,0:T(2,128)(2,1)}), bf16[4,2,49152]{2,1,0:T(2,128)(2,1)S(1)}, u32[]{:S(2)}, u32[]{:S(2)}) async-start(bf16[4,2,49152]{2,1,0:T(2,128)(2,1)} %reshape.568), calls=%async_computation.4 | async-start | bytes 1572864 | tf_op jit(solution)/shard_map/all_to_all | solution.py:153
  (66 other events, 232.6 us)
where the time goes:
time: 374 us; the launch traced here: 367 us
  other arithmetic  105 us (28%)
  local copies, waits for them, and re-layouts  99.3 us (27%)
  blocking collectives  72.3 us (19%)
  between operations  34.9 us (9%)
  starting transfers between devices  29.3 us (8%)
  matrix products  20.4 us (5%)
  waiting for transfers between devices  5.57 us (1%)
    unnamed x10, other arithmetic  52.7 us
    psum x1, blocking collectives, on_device(): gradient = lax.psum(grad_part, ('dp', 'ctx'))  40.7 us
    unnamed x171, local copies, waits for them, and re-layouts  40.3 us
    all_gather x1, blocking collectives, on_device(): lax.all_gather(jnp.stack([adam_mean[0], adam_square[0]]), 'dp', axis=0)  14.3 us
    convert_element_type x1, local copies, waits for them, and re-layouts, norm_backward(): d_y = (d_gated * (gate_f * sigma)).astype(jnp.bfloat16)  13 us
    all_gather x1, blocking collectives, on_device(): lax.all_gather(b_input, 'ctx', axis=1, tiled=True)  9.13 us
    dot_general x3, matrix products, ssd_group(): jnp.einsum('chsn,cshp->chnp', b_decayed, scaled, precision=highest)  8.29 us
    all_gather x1, blocking collectives, on_device(): lax.all_gather(c_input, 'ctx', axis=1, tiled=True)  8.23 us
  transfers between devices with their start and end apart: 7, of which 1 were waited for; matrix products, arithmetic and copies ran while one was open for 19% of the time, Pallas kernels for 0%

commit v1 on v0

--- a/solution.py
+++ b/solution.py
@@ -164,7 +164,7 @@
         jnp.zeros((3, heads_all), jnp.float32), head_grads, (0, first)
     )
     grad_part = jnp.concatenate([full_heads.reshape(-1), d_gain])
-    gradient = lax.psum(grad_part, ("dp", "ctx"))
+    gradient = jnp.sum(lax.all_gather(grad_part, ("dp", "ctx")), 0)
     grad_norm = jnp.sqrt(jnp.sum(gradient * gradient))
     shrink = jnp.minimum(1.0, clip_norm / (grad_norm + 1e-06))
     owners = lax.axis_size("dp")

time: 374 us -> 475 us (1.27)
  waiting for transfers between devices: 5.57 us -> 128 us
  blocking collectives: 72.3 us -> 31.6 us
  between operations: 34.9 us -> 48.2 us
  local copies, waits for them, and re-layouts: 99.3 us -> 105 us
    unnamed x0 -> x2, waiting for transfers between devices: none -> 125 us
    psum x1 -> x0, blocking collectives: 40.7 us -> none  [on_device(): gradient = lax.psum(grad_part, ('dp', 'ctx'))]
    all_to_all x1, waiting for transfers between devices: 5.56 us -> 0.01 us  [on_device(): lax.all_to_all(d_x[None], 'ctx', split_axis=1, concat_axis=2, tiled=True)]
    unnamed x171 -> x176, local copies, waits for them, and re-layouts: 40.3 us -> 43.2 us
    unnamed x10 -> x11, other arithmetic: 52.7 us -> 52.9 us
  transfers between devices with their start and end apart: 7 -> 8, of which waited for: 1 -> 2; matrix products, arithmetic and copies ran while one was open for 19% -> 16% of each run, Pallas kernels for 0% -> 0%
where the time goes in v1:
time: 475 us; the launch traced here: 467 us
  waiting for transfers between devices  128 us (27%)
  local copies, waits for them, and re-layouts  105 us (22%)
  other arithmetic  104 us (22%)
  between operations  48.2 us (10%)
  blocking collectives  31.6 us (7%)
  starting transfers between devices  30.1 us (6%)
  matrix products  20.3 us (4%)
    unnamed x2, waiting for transfers between devices  125 us
    unnamed x11, other arithmetic  52.9 us
    unnamed x176, local copies, waits for them, and re-layouts  43.2 us
    all_gather x1, blocking collectives, on_device(): lax.all_gather(jnp.stack([adam_mean[0], adam_square[0]]), 'dp', axis=0)  14.3 us
    convert_element_type x1, local copies, waits for them, and re-layouts, norm_backward(): d_y = (d_gated * (gate_f * sigma)).astype(jnp.bfloat16)  13 us
  transfers between devices with their start and end apart: 8, of which 2 were waited for; matrix products, arithmetic and copies ran while one was open for 16% of the time, Pallas kernels for 0%

profile of v1, /device:TPU:0, one launch (start us, length us, event | category | flops | bytes accessed | tf_op | source)
XLA Modules:
  0.0 467.4 jit_solution(18158994507360204475)
XLA Ops:
  9.8 5.2 %all-to-all-start.1 = ((bf16[4,2,768]{2,1,0:T(2,128)(2,1)}), bf16[4,2,768]{2,1,0:T(2,128)(2,1)S(1)}, u32[]{:S(2)}, u32[]{:S(2)}) async-start(bf16[4,2,768]{2,1,0:T(2,128)(2,1)} %reshape.563), calls=%async_computation.1 | async-start | bytes 24576 | tf_op jit(solution)/shard_map/all_to_all | solution.py:130
  17.1 9.1 %all_gather.19 = bf16[1,512,128]{2,1,0:T(8,128)(2,1)S(1)} all-gather(bf16[1,128,128]{2,1,0:T(8,128)(2,1)} %param.19), channel_id=1, replica_groups=mesh['dp'=8,'ctx'=4] {'ctx'}, dimensions={1}, use_global_device_ids=true | all-gather | bytes 163840 | tf_op jit(solution)/shard_map/all_gather | solution.py:110
  26.2 8.2 %all_gather.18 = bf16[1,512,128]{2,1,0:T(8,128)(2,1)S(1)} all-gather(bf16[1,128,128]{2,1,0:T(8,128)(2,1)} %param.20), channel_id=1, replica_groups=mesh['dp'=8,'ctx'=4] {'ctx'}, dimensions={1}, use_global_device_ids=true | all-gather | bytes 163840 | tf_op jit(solution)/shard_map/all_gather | solution.py:111
  35.2 3.8 copy.220
  39.0 17.9 %reduce.27 = bf16[3072,128]{1,0:T(8,128)(2,1)} reduce(bf16[3072,1,128]{2,1,0:T(2,128)(2,1)S(1)} %bitcast.223, bf16[]{:T(256)} %broadcast.250), dimensions={1}, to_apply=%bitcast.152.reduce_sub_computation | reduce | bytes 1572866
  58.9 4.4 all-to-all-start
  87.0 6.9 %while.36 = (s32[]{:T(128)}, f32[12,128,64]{2,1,0:T(8,128)S(1)}, f32[2,12,128,64]{3,2,1,0:T(8,128)S(1)}, f32[2,12]{1,0:T(2,128)S(1)}, f32[2,12,1,1]{1,3,2,0:T(1,...) while((s32[]{:T(128)}, f32[12,128,64]{2,1,0:T(8,128)S(1)}, ...), condition=%wide.region_3.4_spmd.clone, body=%wide.region_2.3_spmd.clone.sunk | while | flops 589827 | bytes 5899176 | solution.py:51
  100.5 3.9 copy.238
  104.4 6.3 %reduce.28 = bf16[512,768]{1,0:T(8,128)(2,1)} reduce(bf16[512,1,768]{2,1,0:T(2,128)(2,1)S(1)} %bitcast.217, bf16[]{:T(256)} %broadcast.250), dimensions={1}, to_apply=%bitcast.154.reduce_sub_computation | reduce | bytes 1572866
  112.8 4.5 all-to-all-start.2
  134.0 3.7 reshape.568
  149.7 13.0 %copy.372 = bf16[1,128,3072]{1,0,2:T(2,128)(2,1)} copy(bf16[1,128,3072]{1,2,0:T(8,128)(2,1)S(1)} %get-tuple-element.489) | data formatting | bytes 1572864 | tf_op jit(solution)/shard_map/convert_element_type | solution.py:76
  162.7 18.5 %reduce.29 = bf16[3072,128]{1,0:T(8,128)(2,1)S(1)} reduce(bf16[3072,1,128]{2,1,0:T(2,128)(2,1)} %bitcast.219, bf16[]{:T(256)} %broadcast.250), dimensions={1}, to_apply=%bitcast.190.reduce_sub_computation | reduce | bytes 1572866
  182.2 4.2 all-to-all-start.3
  208.8 14.3 %all-gather.2 = f32[8,2,804]{2,1,0:T(2,128)S(1)} all-gather(f32[1,2,804]{2,1,0:T(2,128)S(1)} %maximum_bitcast_fusion.1), channel_id=2, replica_groups=mesh['dp'=8,'ctx'=4] {'dp'}, dimensions={0}, use_global_device_ids=true | all-gather | bytes 57888 | tf_op jit(solution)/shard_map/all_gather | solution.py:117
  250.9 13.6 %while.37 = (s32[]{:T(128)}, f32[12,128,64]{2,1,0:T(8,128)S(1)}, f32[2,12]{1,0:T(2,128)}, f32[2,12,128,64]{3,2,1,0:T(8,128)}, f32[2,12,128,64]{2,3,1,0:T(8,128)}...) while((s32[]{:T(128)}, f32[12,128,64]{2,1,0:T(8,128)S(1)}, ...), condition=%wide.region_8.9_spmd.clone, body=%wide.region_6.8_spmd.clone.sunk | while | flops 688132 | bytes 4327636 | solution.py:51
  264.6 3.8 fusion.90
  275.9 5.9 %fusion.11 = (f32[2,12,256]{2,1,0:T(8,128)S(1)}, f32[2,12,256]{2,1,0:T(8,128)S(1)}, f32[2,256,256]{2,1,0:T(8,128)}) fusion(bf16[2,12,256,256]{3,2,1,0:T(8,128)(2,1)S(1)} %copy-done.17, f32[2,12,256]{2,1,0:T(8,128)S(1)} %copy-done.38, f32[2,256,256]{2,1,0:T(8,128)} %copy-done.26, pred[256,256]{1,0:T(8,128)(4,1)S(1)} %copy-done.40), kind=kLoop, calls=%fused_computation.26 | loop fusion | flops 18731008 | bytes 4333568 | tf_op jit(solution)/shard_map/transpose(jvp())/reduce_sum | solution.py:36
  281.9 3.8 fusion.13
  286.3 5.0 %reduce-window.31 = f32[2,12,2,128]{3,1,2,0:T(8,128)S(1)} reduce-window(f32[2,12,2,128]{3,1,2,0:T(8,128)S(1)} %copy.261, f32[]{:T(128)} %constant.128.clone.1), window={size=1x1x1x128 pad=0_0x0_0x0_0x0_127}, to_apply=%region_15.16 | reduce-window | flops 780288 | bytes 49156 | tf_op jit(solution)/shard_map/reduce-window.2
  294.6 4.2 all-to-all-start.5
  303.5 5.5 %reduce.30 = bf16[512,768]{1,0:T(8,128)(2,1)S(1)} reduce(bf16[512,1,768]{2,1,0:T(2,128)(2,1)S(1)} %bitcast.221, bf16[]{:T(256)} %broadcast.250), dimensions={1}, to_apply=%bitcast.158.reduce_sub_computation | reduce | bytes 1572866
  313.6 4.2 all-to-all-start.6
  327.7 125.0 %all-reduce.6.cloned.1.call-done = f32[102912]{0:T(1024)} async-done(((f32[102912]{0:T(1024)}), f32[102912]{0:T(1024)}) %all-reduce.6.cloned.1.call-update) | async-done | bytes 411664
  (365 shorter events, 144.7 us)
Async XLA Ops:
  9.8 49.0 %all-to-all-start.1 = ((bf16[4,2,768]{2,1,0:T(2,128)(2,1)}), bf16[4,2,768]{2,1,0:T(2,128)(2,1)S(1)}, u32[]{:S(2)}, u32[]{:S(2)}) async-start(bf16[4,2,768]{2,1,0:T(2,128)(2,1)} %reshape.563), calls=%async_computation.1 | async-start | bytes 24576 | tf_op jit(solution)/shard_map/all_to_all | solution.py:130
  15.9 23.1 %copy-start.75 = (f32[3,12]{1,0:T(4,128)}, f32[3,12]{1,0:T(4,128)S(1)}, u32[]{:S(2)}) copy-start(f32[3,12]{1,0:T(4,128)S(1)} %constant_dynamic-slice_fusion.4) | copy-start | bytes 436
  15.9 47.5 %copy-start.67 = (f32[12]{0:T(128)}, f32[12]{0:T(128)S(1)}, u32[]{:S(2)}) copy-start(f32[12]{0:T(128)S(1)} %get-tuple-element.511) | copy-start | bytes 148
  15.9 47.5 %copy-start.69 = (f32[12]{0:T(128)}, f32[12]{0:T(128)S(1)}, u32[]{:S(2)}) copy-start(f32[12]{0:T(128)S(1)} %get-tuple-element.512) | copy-start | bytes 148
  15.9 80.7 %copy-start.71 = (f32[12]{0:T(128)}, f32[12]{0:T(128)S(1)}, u32[]{:S(2)}) copy-start(f32[12]{0:T(128)S(1)} %get-tuple-element.510) | copy-start | bytes 148
  34.7 35.3 %copy-start.26 = (f32[2,256,256]{2,1,0:T(8,128)}, f32[2,256,256]{2,1,0:T(8,128)S(1)}, u32[]{:S(2)}) copy-start(f32[2,256,256]{2,1,0:T(8,128)S(1)} %fusion.87) | copy-start | bytes 1572868
  34.7 35.3 %copy-start.39 = (pred[256,256]{1,0:T(8,128)(4,1)}, pred[256,256]{1,0:T(8,128)(4,1)S(1)}, u32[]{:S(2)}) copy-start(pred[256,256]{1,0:T(8,128)(4,1)S(1)} %iota_compare_fusion) | copy-start | bytes 196612
  35.1 31.2 %copy-start.28 = (f32[2,256,128]{2,1,0:T(8,128)}, f32[2,256,128]{2,1,0:T(8,128)S(1)}, u32[]{:S(2)}) copy-start(f32[2,256,128]{2,1,0:T(8,128)S(1)} %convert_element_type.229) | copy-start | bytes 786436
  35.2 33.0 %copy-start.30 = (f32[2,256,128]{2,1,0:T(8,128)}, f32[2,256,128]{2,1,0:T(8,128)S(1)}, u32[]{:S(2)}) copy-start(f32[2,256,128]{2,1,0:T(8,128)S(1)} %convert_element_type.232) | copy-start | bytes 786436
  58.9 14.0 %all-to-all-start = ((bf16[4,2,49152]{2,1,0:T(2,128)(2,1)}), bf16[4,2,49152]{2,1,0:T(2,128)(2,1)}, u32[]{:S(2)}, u32[]{:S(2)}) async-start(bf16[4,2,49152]{2,1,0:T(2,128)(2,1)} %reshape.565), calls=%async_computation | async-start | bytes 1572864 | tf_op jit(solution)/shard_map/all_to_all | solution.py:129
  63.5 19.5 %copy-start.45 = (f32[2,256,12]{1,2,0:T(8,128)}, f32[2,256,12]{1,2,0:T(8,128)S(1)}, u32[]{:S(2)}) copy-start(f32[2,256,12]{1,2,0:T(8,128)S(1)} %get-tuple-element.503) | copy-start | bytes 73732
  112.8 21.3 %all-to-all-start.2 = ((bf16[4,2,49152]{2,1,0:T(2,128)(2,1)}), bf16[4,2,49152]{2,1,0:T(2,128)(2,1)}, u32[]{:S(2)}, u32[]{:S(2)}) async-start(bf16[4,2,49152]{2,1,0:T(2,128)(2,1)} %reshape.567), calls=%async_computation.2 | async-start | bytes 1572864 | tf_op jit(solution)/shard_map/all_to_all | solution.py:142
  181.1 27.6 %copy-start.65 = (f32[1,804]{1,0:T(1,128)S(1)}, f32[1,804]{1,0:T(1,128)}, u32[]{:S(2)}) copy-start(f32[1,804]{1,0:T(1,128)} %param.25) | copy-start | bytes 9652
  181.1 27.6 %copy-start.66 = (f32[1,804]{1,0:T(1,128)S(1)}, f32[1,804]{1,0:T(1,128)}, u32[]{:S(2)}) copy-start(f32[1,804]{1,0:T(1,128)} %param.24) | copy-start | bytes 9652
  182.2 50.9 %all-to-all-start.3 = ((bf16[4,2,49152]{2,1,0:T(2,128)(2,1)}), bf16[4,2,49152]{2,1,0:T(2,128)(2,1)S(1)}, u32[]{:S(2)}, u32[]{:S(2)}) async-start(bf16[4,2,49152]{2,1,0:T(2,128)(2,1)} %reshape.569), calls=%async_computation.3 | async-start | bytes 1572864 | tf_op jit(solution)/shard_map/all_to_all | solution.py:149
  285.7 13.4 %copy-start.33 = (bf16[1,512,128]{2,1,0:T(8,128)(2,1)S(1)}, bf16[1,512,128]{2,1,0:T(8,128)(2,1)}, u32[]{:S(2)}) copy-start(bf16[1,512,128]{2,1,0:T(8,128)(2,1)} %copy-done.32) | copy-start | bytes 393220
  294.6 19.0 %all-to-all-start.5 = ((bf16[4,2,768]{2,1,0:T(2,128)(2,1)}), bf16[4,2,768]{2,1,0:T(2,128)(2,1)S(1)}, u32[]{:S(2)}, u32[]{:S(2)}) async-start(bf16[4,2,768]{2,1,0:T(2,128)(2,1)} %reshape.573), calls=%async_computation.5 | async-start | bytes 24576 | tf_op jit(solution)/shard_map/all_to_all | solution.py:154
  313.6 9.6 %all-to-all-start.6 = ((bf16[4,2,16384]{2,1,0:T(2,128)(2,1)}), bf16[4,2,16384]{2,1,0:T(2,128)(2,1)S(1)}, u32[]{:S(2)}, u32[]{:S(2)}) async-start(bf16[4,2,16384]{2,1,0:T(2,128)(2,1)} %reshape.575), calls=%async_computation.6 | async-start | bytes 524288 | tf_op jit(solution)/shard_map/all_to_all | solution.py:155
  317.8 134.9 %all-reduce.6.cloned.1.call-start = ((), (), s32[]{:S(2)}) async-start(), calls=%async_computation.7 | async-start | bytes 827392
  323.1 134.7 %all-to-all-start.4 = ((bf16[4,2,49152]{2,1,0:T(2,128)(2,1)}), bf16[4,2,49152]{2,1,0:T(2,128)(2,1)S(1)}, u32[]{:S(2)}, u32[]{:S(2)}) async-start(bf16[4,2,49152]{2,1,0:T(2,128)(2,1)} %reshape.571), calls=%async_computation.4 | async-start | bytes 1572864 | tf_op jit(solution)/shard_map/all_to_all | solution.py:153
  326.6 128.7 %copy-start.63 = (f32[804]{0:T(1024)S(1)}, f32[804]{0:T(1024)}, u32[]{:S(2)}) copy-start(f32[804]{0:T(1024)} %get-tuple-element.532) | copy-start | bytes 9652
  326.6 128.7 %copy-start.64 = (f32[804]{0:T(1024)S(1)}, f32[804]{0:T(1024)}, u32[]{:S(2)}) copy-start(f32[804]{0:T(1024)} %get-tuple-element.533) | copy-start | bytes 9652
  326.7 130.6 %copy-start.54 = (f32[3216]{0:T(1024)S(1)}, f32[3216]{0:T(1024)}, u32[]{:S(2)}) copy-start(f32[3216]{0:T(1024)} %get-tuple-element.445) | copy-start | bytes 38596
  326.7 130.6 %copy-start.56 = (f32[3216]{0:T(1024)S(1)}, f32[3216]{0:T(1024)}, u32[]{:S(2)}) copy-start(f32[3216]{0:T(1024)} %param.23) | copy-start | bytes 38596
  (69 other events, 268.9 us)
Sparse Core Ops, SparseCore 0:
  323.9 128.7 all-reduce.5
